TPU v7x, 128 devices: a whole 4x4x4 slice. The times are simulated.
128 devices in a mesh: gx: 16 (over y_hi, z, core), gy: 8 (over x, y_lo).
Axes of the slice: x: 4, y: 4 (y_hi: 2, y_lo: 2; y = y_hi * 2 + y_lo), z: 4, core: 2. Of those that a mesh axis runs over, the one named last changes fastest.
Arguments:
- payload: float32 [4, 2097152], P(None, ('gx', 'gy'))
- cells: int32 [3, 2097152], P(None, ('gx', 'gy')), may hold values from 0 to 127, as said below
- counts: int32 [128, 9], P(('gx', 'gy')), may hold values from 128 to 12596, as said below
Outputs:
- scalar_field: float32 [8, 256, 1024], P(None, 'gx', 'gy')
- momentum: float32 [3, 8, 256, 1024], P(None, None, 'gx', 'gy')
Inputs may be any that keep to these rules, and one draw needn't show every extreme that they name: Rows of a tile are grouped by direction in the order of counts' columns. A face direction holds at most 2048 rows of a tile and a corner direction at most 512; each of these bounds is reached in some tile. A row of counts sums to 16384. cells[0] is below 8, cells[1] below 16, cells[2] below 128. A particle moving +x lands in x layers 0 to 1 of its destination tile, one moving -x in layers 14 to 15; likewise +y in y layers 0 to 15 and -y in 112 to 127; corner directions are bound in both; otherwise any cell.
All inputs are finite; a program needn't handle non-finite values.
Results may differ from a plain program's by a relative error of at most 0.000054.
Values sent between devices are 32-bit elements; how exact they have to be, the bound alone decides.
No kernel may reach another device: no remote copies, remote signals or barrier semaphores. Data moves between devices by JAX's collectives and lax.ppermute only.
A program may use at most 64 MiB of HBM per device.

v0:
```python
import jax
import jax.numpy as jnp
from jax import lax
from jax.experimental import pallas as pl
from jax.experimental.pallas import tpu as pltpu
from jax.sharding import PartitionSpec as P

CX = 16
CY = 128
NZ = 8
SWEEPS = 4
PART = 16384
CAP_F = 2048
CAP_D = 512


SCREENING = 0.5
CUBIC_TERM = 0.3
COUPLING = 1.5
SMOOTHING = 0.1
BACKGROUND = 1.0

HALO = 2 * SWEEPS
ROWS = 64
COLS = 256
SPLITS = 3
BLOCK = 2048
WIDE_X = 2 * CX
WIDE_Y = 2 * CY

STEPS = ((1, 0), (-1, 0), (0, 1), (0, -1), (1, 1), (1, -1), (-1, 1), (-1, -1))


def deposit_body(first_ref, p_ref, c_ref, acc_ref, o_ref):
    step = pl.program_id(0)

    @pl.when(step == 0)
    def _():
        if acc_ref is None:
            o_ref[...] = jnp.zeros(o_ref.shape, o_ref.dtype)
        else:
            o_ref[...] = acc_ref[...]

    @pl.when(step * BLOCK + BLOCK > first_ref[0])
    def _():
        p = p_ref[...].astype(jnp.float32)
        c = c_ref[...].astype(jnp.int32)
        width = p.shape[1]
        masses = p[0:1]
        vals = jnp.concatenate([masses, masses * p[1:4]], axis=0)
        cell = (c[0:1] * CX + c[1:2]) * CY + c[2:3]
        position = step * BLOCK + lax.broadcasted_iota(jnp.int32, (1, width), 1)
        cell = jnp.where(position >= first_ref[0], cell, -1)
        row = lax.shift_right_arithmetic(cell, 8)
        col = lax.bitwise_and(cell, COLS - 1)
        hi = vals.astype(jnp.bfloat16)
        rest = vals - hi.astype(jnp.float32)
        mid = rest.astype(jnp.bfloat16)
        lo = (rest - mid.astype(jnp.float32)).astype(jnp.bfloat16)
        parts = [q.astype(jnp.float32)[e : e + 1] for q in (hi, mid, lo) for e in range(4)]
        row_hot = (lax.broadcasted_iota(jnp.int32, (ROWS, width), 0) == row).astype(jnp.float32)
        left = jnp.concatenate([(row_hot * part).astype(jnp.bfloat16) for part in parts], axis=0)
        right = (lax.broadcasted_iota(jnp.int32, (COLS, width), 0) == col).astype(jnp.bfloat16)
        o_ref[...] += lax.dot_general(
            left, right, (((1,), (1,)), ((), ())), preferred_element_type=jnp.float32
        )


def deposit(values, targets, first, acc=None):
    count = values.shape[1] // BLOCK
    shape = (4 * SPLITS * ROWS, COLS)
    pick = lambda b, f: (0, jnp.maximum(b, f[0] // BLOCK))
    in_specs = [pl.BlockSpec((4, BLOCK), pick), pl.BlockSpec((3, BLOCK), pick)]
    operands = [first, values, targets]
    aliases = {}
    if acc is None:
        kernel = lambda f, p, c, o: deposit_body(f, p, c, None, o)
    else:
        kernel = deposit_body
        in_specs.append(pl.BlockSpec(shape, lambda b, f: (0, 0)))
        operands.append(acc)
        aliases = {3: 0}
    return pl.pallas_call(
        kernel,
        grid_spec=pltpu.PrefetchScalarGridSpec(
            num_scalar_prefetch=1,
            grid=(count,),
            in_specs=in_specs,
            out_specs=pl.BlockSpec(shape, lambda b, f: (0, 0)),
        ),
        out_shape=jax.ShapeDtypeStruct(shape, jnp.float32),
        input_output_aliases=aliases,
        compiler_params=pltpu.CompilerParams(dimension_semantics=("arbitrary",)),
    )(*operands)


def combine(total):
    total = total.reshape(SPLITS, 4, ROWS * COLS)
    summed = (total[0] + total[1]) + total[2]
    return summed.reshape(4, NZ, CX, CY)


def shifted(block, axis, route_to):
    count = lax.axis_size(axis)
    return lax.ppermute(block, axis, [(i, (i + route_to) % count) for i in range(count)])


def bordered_density(density):
    head = density[:, :HALO, :]
    tail = density[:, CX - HALO :, :]
    wide = jnp.concatenate([density, shifted(head, "gx", -1), shifted(tail, "gx", 1)], axis=1)
    head = wide[:, :, :HALO]
    tail = wide[:, :, CY - HALO :]
    gap = jnp.zeros((NZ, WIDE_X, WIDE_Y - CY - 2 * HALO), jnp.float32)
    return jnp.concatenate([wide, shifted(head, "gy", -1), gap, shifted(tail, "gy", 1)], axis=2)


def near(v):
    flat = jnp.zeros((1,) + v.shape[1:], v.dtype)
    up = jnp.concatenate([v[1:], flat], axis=0)
    down = jnp.concatenate([flat, v[:-1]], axis=0)
    return (
        up
        + down
        + pltpu.roll(v, WIDE_X - 1, 1)
        + pltpu.roll(v, 1, 1)
        + pltpu.roll(v, WIDE_Y - 1, 2)
        + pltpu.roll(v, 1, 2)
    )


def relax_kernel(d_ref, o_ref):
    density = d_ref[...]
    source = COUPLING * ((density + SMOOTHING * (near(density) - 6.0 * density)) - BACKGROUND)
    shape = density.shape
    parity = (
        lax.broadcasted_iota(jnp.int32, shape, 0)
        + lax.broadcasted_iota(jnp.int32, shape, 1)
        + lax.broadcasted_iota(jnp.int32, shape, 2)
    ) % 2
    field = jnp.zeros(shape, jnp.float32)
    for sweep_no in range(SWEEPS):
        for colour in (0, 1):
            middle = field
            residual = (
                near(middle)
                - 6.0 * middle
                - SCREENING * middle
                - CUBIC_TERM * middle * middle * middle
                - source
            )
            slope = -6.0 - SCREENING - 3.0 * CUBIC_TERM * middle * middle
            field = jnp.where(parity == colour, middle - residual / slope, middle)
    o_ref[...] = field[:, :CX, :CY]


def relax(bordered):
    return pl.pallas_call(
        relax_kernel,
        out_shape=jax.ShapeDtypeStruct((NZ, CX, CY), jnp.float32),
    )(bordered)


def shards(payload, cells, counts):
    tallies = counts[0]
    limits = jnp.cumsum(tallies)
    starts = limits - tallies
    packed = jnp.concatenate([payload, cells.astype(jnp.float32)], axis=0)

    gx = lax.axis_size("gx")
    gy = lax.axis_size("gy")
    sends = []
    for which, (sx, sy) in enumerate(STEPS):
        capacity = CAP_F if which < 4 else CAP_D
        block = lax.dynamic_slice_in_dim(packed, starts[which], capacity, 1)
        living = (jnp.arange(capacity, dtype=jnp.int32) < tallies[which]).astype(jnp.float32)
        block = jnp.concatenate([block[0:1] * living[None, :], block[1:]], axis=0)
        route = []
        for ix in range(gx):
            for iy in range(gy):
                route.append((ix * gy + iy, ((ix + sx) % gx) * gy + (iy + sy) % gy))
        sends.append(lax.ppermute(block, ("gx", "gy"), route))

    total = deposit(payload, cells, starts[8].reshape(1))
    arrived = jnp.concatenate(sends, axis=1)
    total = deposit(arrived[0:4], arrived[4:7], jnp.zeros((1,), jnp.int32), total)
    interior = combine(total)
    density = interior[0]
    momentum = interior[1:]
    scalar_field = relax(bordered_density(density))
    return (scalar_field, momentum)


def solution(mesh):
    placed = (P(None, ("gx", "gy")), P(None, ("gx", "gy")), P(("gx", "gy"), None))
    return jax.shard_map(
        shards,
        mesh=mesh,
        in_specs=placed,
        out_specs=(P(None, "gx", "gy"), P(None, None, "gx", "gy")),
        check_vma=False,
    )
```

profile of v0, /device:TPU:0, one launch (start us, length us, event | category | flops | bytes accessed | tf_op | source)
XLA Modules:
  0.0 92.7 jit_solution(14027013360565595700)
XLA Ops:
  1.5 0.7 fusion.10
  7.7 1.0 %convert_element_type.19 = f32[3,16384]{1,0:T(4,128)S(1)} convert(s32[3,16384]{1,0:T(4,128)} %c.1) | non-fusion elementwise | flops 49152 | bytes 393216 | tf_op jit(solution)/shard_map/convert_element_type | solution.py:168
  12.1 6.3 %collective-permute-start.1 = (f32[7,2048]{1,0:T(8,128)S(1)}, f32[7,2048]{1,0:T(8,128)S(1)}, u32[]{:S(2)}, u32[]{:S(2)}) collective-permute-start(f32[7,2048]{1,0:T(8,128)S(1)} %pad_maximum_fusion.2), channel_id=1, source_target_pairs={{0,120},{1,121},{2,122},{3,123},{4,124},{5,125},{6,126},{7,127},{8... | collective-permute-start | bytes 172040 | tf_op jit(solution)/shard_map/ppermute | solution.py:182
  18.4 0.7 compare_select_fusion.3
  19.9 0.7 collective-permute-start.2
  20.7 0.7 compare_select_fusion
  21.4 3.5 %collective-permute-start.3 = (f32[7,2048]{1,0:T(8,128)S(1)}, f32[7,2048]{1,0:T(8,128)S(1)}, u32[]{:S(2)}, u32[]{:S(2)}) collective-permute-start(f32[7,2048]{1,0:T(8,128)S(1)} %pad_maximum_fusion.4), channel_id=1, source_target_pairs={{0,7},{1,0},{2,1},{3,2},{4,3},{5,4},{6,5},{7,6},{8,15},{9,8},{10,9... | collective-permute-start | bytes 172040 | tf_op jit(solution)/shard_map/ppermute | solution.py:182
  33.5 0.7 compare_select_fusion.6
  35.5 6.8 %shard_map.50.acc_ref = f32[768,256]{1,0:T(8,128)} custom-call(s32[1]{0:T(128)} %get-tuple-element.14.f, f32[4,16384]{1,0:T(4,128)} %p.1, s32[3,16384]{1,0:T(4,128)} %c.1), custom_call_target="tpu_custom_call" | custom-call | tf_op jit(solution)/shard_map/pallas_call | solution.py:83
  43.0 5.3 %collective-permute-start.6 = (f32[7,512]{1,0:T(8,128)S(1)}, f32[7,512]{1,0:T(8,128)S(1)}, u32[]{:S(2)}, u32[]{:S(2)}) collective-permute-start(f32[7,512]{1,0:T(8,128)S(1)} %pad_maximum_fusion.7), channel_id=1, source_target_pairs={{0,121},{1,122},{2,123},{3,124},{4,125},{5,126},{6,127},{7,120},{8... | collective-permute-start | bytes 43016 | tf_op jit(solution)/shard_map/ppermute | solution.py:182
  48.3 6.3 %collective-permute-start.7 = (f32[7,512]{1,0:T(8,128)S(1)}, f32[7,512]{1,0:T(8,128)S(1)}, u32[]{:S(2)}, u32[]{:S(2)}) collective-permute-start(f32[7,512]{1,0:T(8,128)S(1)} %pad_maximum_fusion.8), channel_id=1, source_target_pairs={{0,127},{1,120},{2,121},{3,122},{4,123},{5,124},{6,125},{7,126},{8... | collective-permute-start | bytes 43016 | tf_op jit(solution)/shard_map/ppermute | solution.py:182
  54.7 1.4 %collective-permute-done.7 = f32[7,512]{1,0:T(8,128)S(1)} collective-permute-done((f32[7,512]{1,0:T(8,128)S(1)}, f32[7,512]{1,0:T(8,128)S(1)}, u32[]{:S(2)}, u32[]{:S(2)}) %collective-permute-start.7) | collective-permute-done | bytes 14368 | tf_op jit(solution)/shard_map/ppermute | solution.py:182
  56.1 0.7 slice.210.p_ref
  56.8 0.7 slice.211.c_ref
  57.5 7.4 %shard_map.51 = f32[768,256]{1,0:T(8,128)} custom-call(s32[1]{0:T(128)} %constant.15.clone.1.first_ref, f32[4,10240]{1,0:T(4,128)} %slice.210.p_ref, f32[3,10240]{1,0:T(4,128)} %slice.211.c_ref, f32[768,256]{1,0:T(8,128)} %shard_map.50.acc_ref), custom_call_target="tpu_custom_call", output_to_operand_aliasing={{}: (3, {})} | custom-call | tf_op jit(solution)/shard_map/pallas_call | solution.py:83
  64.9 1.2 %slice_add_fusion = f32[256,256]{1,0:T(8,128)S(1)} fusion(f32[768,256]{1,0:T(8,128)} %shard_map.51), kind=kLoop, calls=%fused_computation.16 | loop fusion | flops 131072 | bytes 1048576 | tf_op jit(solution)/shard_map/add | solution.py:99
  66.1 0.8 collective-permute-start.8
  66.9 1.6 %collective-permute-done.8 = f32[8,8,128]{2,1,0:T(8,128)S(1)} collective-permute-done((f32[8,8,128]{2,1,0:T(8,128)S(1)}, f32[8,8,128]{2,1,0:T(8,128)S(1)}, u32[]{:S(2)}, u32[]{:S(2)}) %collective-permute-start.8) | collective-permute-done | bytes 32800 | tf_op jit(solution)/shard_map/ppermute | solution.py:105
  68.5 5.4 %collective-permute-done.9 = f32[8,8,128]{2,1,0:T(8,128)S(1)} collective-permute-done((f32[8,8,128]{2,1,0:T(8,128)S(1)}, f32[8,8,128]{2,1,0:T(8,128)S(1)}, u32[]{:S(2)}, u32[]{:S(2)}) %collective-permute-start.9) | collective-permute-done | bytes 32800 | tf_op jit(solution)/shard_map/ppermute | solution.py:105
  74.0 7.3 %collective-permute-start.10 = (f32[8,32,8]{2,1,0:T(8,128)S(1)}, f32[8,32,8]{2,1,0:T(8,128)S(1)}, u32[]{:S(2)}, u32[]{:S(2)}) collective-permute-start(f32[8,32,8]{2,1,0:T(8,128)S(1)} %get-tuple-element.10), channel_id=1, source_target_pairs={{0,7},{1,0},{2,1},{3,2},{4,3},{5,4},{6,5},{7,6},{8,15},{9,8},{10,9... | collective-permute-start | bytes 24584 | tf_op jit(solution)/shard_map/ppermute | solution.py:105
  82.1 1.7 %collective-permute-done.10 = f32[8,32,8]{2,1,0:T(8,128)S(1)} collective-permute-done((f32[8,32,8]{2,1,0:T(8,128)S(1)}, f32[8,32,8]{2,1,0:T(8,128)S(1)}, u32[]{:S(2)}, u32[]{:S(2)}) %collective-permute-start.10) | collective-permute-done | bytes 8224 | tf_op jit(solution)/shard_map/ppermute | solution.py:105
  83.8 4.6 %collective-permute-done.11 = f32[8,32,8]{2,1,0:T(8,128)S(1)} collective-permute-done((f32[8,32,8]{2,1,0:T(8,128)S(1)}, f32[8,32,8]{2,1,0:T(8,128)S(1)}, u32[]{:S(2)}, u32[]{:S(2)}) %collective-permute-start.11) | collective-permute-done | bytes 8224 | tf_op jit(solution)/shard_map/ppermute | solution.py:105
  88.4 0.8 pad_maximum_fusion.d_ref
  89.2 3.6 %shard_map.52 = f32[8,16,128]{2,1,0:T(8,128)} custom-call(f32[8,32,256]{2,1,0:T(8,128)} %pad_maximum_fusion.d_ref), custom_call_target="tpu_custom_call" | custom-call | tf_op jit(solution)/shard_map/pallas_call | solution.py:158
  (61 shorter events, 6.9 us)
Async XLA Ops:
  0.6 0.7 copy-start.1
  7.7 3.5 %copy-start = (f32[4,16384]{1,0:T(4,128)S(1)}, f32[4,16384]{1,0:T(4,128)}, u32[]{:S(2)}) copy-start(f32[4,16384]{1,0:T(4,128)} %p.1) | copy-start | bytes 786436
  12.1 30.9 %collective-permute-start.1 = (f32[7,2048]{1,0:T(8,128)S(1)}, f32[7,2048]{1,0:T(8,128)S(1)}, u32[]{:S(2)}, u32[]{:S(2)}) collective-permute-start(f32[7,2048]{1,0:T(8,128)S(1)} %pad_maximum_fusion.2), channel_id=1, source_target_pairs={{0,120},{1,121},{2,122},{3,123},{4,124},{5,125},{6,126},{7,127},{8... | collective-permute-start | bytes 172040 | tf_op jit(solution)/shard_map/ppermute | solution.py:182
  19.1 23.2 %collective-permute-start = (f32[7,2048]{1,0:T(8,128)S(1)}, f32[7,2048]{1,0:T(8,128)S(1)}, u32[]{:S(2)}, u32[]{:S(2)}) collective-permute-start(f32[7,2048]{1,0:T(8,128)S(1)} %pad_maximum_fusion.1), channel_id=1, source_target_pairs={{0,8},{1,9},{2,10},{3,11},{4,12},{5,13},{6,14},{7,15},{8,16},{9,17... | collective-permute-start | bytes 172040 | tf_op jit(solution)/shard_map/ppermute | solution.py:182
  19.9 28.4 %collective-permute-start.2 = (f32[7,2048]{1,0:T(8,128)S(1)}, f32[7,2048]{1,0:T(8,128)S(1)}, u32[]{:S(2)}, u32[]{:S(2)}) collective-permute-start(f32[7,2048]{1,0:T(8,128)S(1)} %pad_maximum_fusion.3), channel_id=1, source_target_pairs={{0,1},{1,2},{2,3},{3,4},{4,5},{5,6},{6,7},{7,0},{8,9},{9,10},{10,1... | collective-permute-start | bytes 172040 | tf_op jit(solution)/shard_map/ppermute | solution.py:182
  21.4 33.2 %collective-permute-start.3 = (f32[7,2048]{1,0:T(8,128)S(1)}, f32[7,2048]{1,0:T(8,128)S(1)}, u32[]{:S(2)}, u32[]{:S(2)}) collective-permute-start(f32[7,2048]{1,0:T(8,128)S(1)} %pad_maximum_fusion.4), channel_id=1, source_target_pairs={{0,7},{1,0},{2,1},{3,2},{4,3},{5,4},{6,5},{7,6},{8,15},{9,8},{10,9... | collective-permute-start | bytes 172040 | tf_op jit(solution)/shard_map/ppermute | solution.py:182
  33.4 21.3 %collective-permute-start.4 = (f32[7,512]{1,0:T(8,128)S(1)}, f32[7,512]{1,0:T(8,128)S(1)}, u32[]{:S(2)}, u32[]{:S(2)}) collective-permute-start(f32[7,512]{1,0:T(8,128)S(1)} %pad_maximum_fusion.5), channel_id=1, source_target_pairs={{0,9},{1,10},{2,11},{3,12},{4,13},{5,14},{6,15},{7,8},{8,17},{9,18... | collective-permute-start | bytes 43016 | tf_op jit(solution)/shard_map/ppermute | solution.py:182
  42.4 12.3 %collective-permute-start.5 = (f32[7,512]{1,0:T(8,128)S(1)}, f32[7,512]{1,0:T(8,128)S(1)}, u32[]{:S(2)}, u32[]{:S(2)}) collective-permute-start(f32[7,512]{1,0:T(8,128)S(1)} %pad_maximum_fusion.6), channel_id=1, source_target_pairs={{0,15},{1,8},{2,9},{3,10},{4,11},{5,12},{6,13},{7,14},{8,23},{9,16... | collective-permute-start | bytes 43016 | tf_op jit(solution)/shard_map/ppermute | solution.py:182
  43.0 11.7 %collective-permute-start.6 = (f32[7,512]{1,0:T(8,128)S(1)}, f32[7,512]{1,0:T(8,128)S(1)}, u32[]{:S(2)}, u32[]{:S(2)}) collective-permute-start(f32[7,512]{1,0:T(8,128)S(1)} %pad_maximum_fusion.7), channel_id=1, source_target_pairs={{0,121},{1,122},{2,123},{3,124},{4,125},{5,126},{6,127},{7,120},{8... | collective-permute-start | bytes 43016 | tf_op jit(solution)/shard_map/ppermute | solution.py:182
  48.3 7.7 %collective-permute-start.7 = (f32[7,512]{1,0:T(8,128)S(1)}, f32[7,512]{1,0:T(8,128)S(1)}, u32[]{:S(2)}, u32[]{:S(2)}) collective-permute-start(f32[7,512]{1,0:T(8,128)S(1)} %pad_maximum_fusion.8), channel_id=1, source_target_pairs={{0,127},{1,120},{2,121},{3,122},{4,123},{5,124},{6,125},{7,126},{8... | collective-permute-start | bytes 43016 | tf_op jit(solution)/shard_map/ppermute | solution.py:182
  66.1 2.4 %collective-permute-start.8 = (f32[8,8,128]{2,1,0:T(8,128)S(1)}, f32[8,8,128]{2,1,0:T(8,128)S(1)}, u32[]{:S(2)}, u32[]{:S(2)}) collective-permute-start(f32[8,8,128]{2,1,0:T(8,128)S(1)} %get-tuple-element.13), channel_id=1, source_target_pairs={{0,120},{8,0},{16,8},{24,16},{32,24},{40,32},{48,40},{56,48},{64,5... | collective-permute-start | bytes 98312 | tf_op jit(solution)/shard_map/ppermute | solution.py:105
  66.9 7.0 %collective-permute-start.9 = (f32[8,8,128]{2,1,0:T(8,128)S(1)}, f32[8,8,128]{2,1,0:T(8,128)S(1)}, u32[]{:S(2)}, u32[]{:S(2)}) collective-permute-start(f32[8,8,128]{2,1,0:T(8,128)S(1)} %get-tuple-element.12), channel_id=1, source_target_pairs={{0,8},{8,16},{16,24},{24,32},{32,40},{40,48},{48,56},{56,64},{64,7... | collective-permute-start | bytes 98312 | tf_op jit(solution)/shard_map/ppermute | solution.py:105
  74.0 9.8 %collective-permute-start.10 = (f32[8,32,8]{2,1,0:T(8,128)S(1)}, f32[8,32,8]{2,1,0:T(8,128)S(1)}, u32[]{:S(2)}, u32[]{:S(2)}) collective-permute-start(f32[8,32,8]{2,1,0:T(8,128)S(1)} %get-tuple-element.10), channel_id=1, source_target_pairs={{0,7},{1,0},{2,1},{3,2},{4,3},{5,4},{6,5},{7,6},{8,15},{9,8},{10,9... | collective-permute-start | bytes 24584 | tf_op jit(solution)/shard_map/ppermute | solution.py:105
  81.3 7.1 %collective-permute-start.11 = (f32[8,32,8]{2,1,0:T(8,128)S(1)}, f32[8,32,8]{2,1,0:T(8,128)S(1)}, u32[]{:S(2)}, u32[]{:S(2)}) collective-permute-start(f32[8,32,8]{2,1,0:T(8,128)S(1)} %get-tuple-element.11), channel_id=1, source_target_pairs={{0,1},{1,2},{2,3},{3,4},{4,5},{5,6},{6,7},{7,0},{8,9},{9,10},{10,1... | collective-permute-start | bytes 24584 | tf_op jit(solution)/shard_map/ppermute | solution.py:105
where the time goes:
time: 93.3 us; the launch traced here: 92.7 us
  starting transfers between devices  31.1 us (33%)
  Pallas kernels  17.8 us (19%)
  between operations  16 us (17%)
  waiting for transfers between devices  14.6 us (16%)
  other arithmetic  8.86 us (9%)
  local copies, waits for them, and re-layouts  4.43 us (5%)
    ppermute x8, starting transfers between devices, shards(): sends.append(lax.ppermute(block, ('gx', 'gy'), route))  22.9 us
    pallas_call x2, Pallas kernels, deposit(): pl.pallas_call(kernel, grid_spec=pltpu.PrefetchScalarGridSpec(num_scalar_...  14.2 us
    ppermute x4, waiting for transfers between devices, shifted(): lax.ppermute(block, axis, [(i, (i + route_to) % count) for i in range(cou...  13.2 us
    ppermute x4, starting transfers between devices, shifted(): lax.ppermute(block, axis, [(i, (i + route_to) % count) for i in range(cou...  8.15 us
    mul x8, other arithmetic, shards(): block = jnp.concatenate([block[0:1] * living[None, :], block[1:]], axis=0)  5.23 us
    pallas_call x1, Pallas kernels, relax(): pl.pallas_call(relax_kernel, out_shape=jax.ShapeDtypeStruct((NZ, CX, CY),...  3.56 us
  transfers between devices with their start and end apart: 12, of which 5 were waited for; matrix products, arithmetic and copies ran while one was open for 6% of the time, Pallas kernels for 7%

commit v1 on v0

--- a/solution.py
+++ b/solution.py
@@ -25,14 +25,28 @@
 COLS = 256
 SPLITS = 3
 BLOCK = 2048
+LANE = 128
+ARRIVED_BLOCK = (4 * CAP_F + 4 * CAP_D + 8 * LANE) // 4
 WIDE_X = 2 * CX
 WIDE_Y = 2 * CY
 
 STEPS = ((1, 0), (-1, 0), (0, 1), (0, -1), (1, 1), (1, -1), (-1, 1), (-1, -1))
 
 
-def deposit_body(first_ref, p_ref, c_ref, acc_ref, o_ref):
+def local_start(count_ref):
+    total = count_ref[0, 0]
+    for edge in range(1, 8):
+        total = total + count_ref[0, edge]
+    return total
+
+
+def no_start(count_ref):
+    return 0
+
+
+def deposit_body(first_of, block, first_ref, p_ref, c_ref, acc_ref, o_ref):
     step = pl.program_id(0)
+    first = first_of(first_ref)
 
     @pl.when(step == 0)
     def _():
@@ -41,7 +55,7 @@
         else:
             o_ref[...] = acc_ref[...]
 
-    @pl.when(step * BLOCK + BLOCK > first_ref[0])
+    @pl.when(step * block + block > first)
     def _():
         p = p_ref[...].astype(jnp.float32)
         c = c_ref[...].astype(jnp.int32)
@@ -49,8 +63,8 @@
         masses = p[0:1]
         vals = jnp.concatenate([masses, masses * p[1:4]], axis=0)
         cell = (c[0:1] * CX + c[1:2]) * CY + c[2:3]
-        position = step * BLOCK + lax.broadcasted_iota(jnp.int32, (1, width), 1)
-        cell = jnp.where(position >= first_ref[0], cell, -1)
+        position = step * block + lax.broadcasted_iota(jnp.int32, (1, width), 1)
+        cell = jnp.where(position >= first, cell, -1)
         row = lax.shift_right_arithmetic(cell, 8)
         col = lax.bitwise_and(cell, COLS - 1)
         hi = vals.astype(jnp.bfloat16)
@@ -66,17 +80,17 @@
         )
 
 
-def deposit(values, targets, first, acc=None):
-    count = values.shape[1] // BLOCK
+def deposit(values, targets, first, first_of, block, acc=None):
+    count = values.shape[1] // block
     shape = (4 * SPLITS * ROWS, COLS)
-    pick = lambda b, f: (0, jnp.maximum(b, f[0] // BLOCK))
-    in_specs = [pl.BlockSpec((4, BLOCK), pick), pl.BlockSpec((3, BLOCK), pick)]
+    pick = lambda b, f: (0, jnp.maximum(b, first_of(f) // block))
+    in_specs = [pl.BlockSpec((4, block), pick), pl.BlockSpec((3, block), pick)]
     operands = [first, values, targets]
     aliases = {}
     if acc is None:
-        kernel = lambda f, p, c, o: deposit_body(f, p, c, None, o)
+        kernel = lambda f, p, c, o: deposit_body(first_of, block, f, p, c, None, o)
     else:
-        kernel = deposit_body
+        kernel = lambda f, p, c, a, o: deposit_body(first_of, block, f, p, c, a, o)
         in_specs.append(pl.BlockSpec(shape, lambda b, f: (0, 0)))
         operands.append(acc)
         aliases = {3: 0}
@@ -94,25 +108,69 @@
     )(*operands)
 
 
+def pack_kernel(count_ref, p_ref, c_ref, *out_refs):
+    start = 0
+    for which, out_ref in enumerate(out_refs):
+        tally = count_ref[0, which]
+        width = out_ref.shape[1]
+        base = pl.multiple_of((start // LANE) * LANE, LANE)
+        offset = start - base
+        p = p_ref[:, pl.ds(base, width)]
+        c = c_ref[:, pl.ds(base, width)]
+        lane = lax.broadcasted_iota(jnp.int32, (1, width), 1)
+        living = (lane >= offset) & (lane < offset + tally)
+        out_ref[0:1, :] = jnp.where(living, p[0:1], 0.0)
+        out_ref[1:4, :] = p[1:4]
+        out_ref[4:7, :] = c.astype(jnp.float32)
+        start = start + tally
+
+
+def pack(payload, cells, counts):
+    widths = [(CAP_F if which < 4 else CAP_D) + LANE for which in range(8)]
+    return pl.pallas_call(
+        pack_kernel,
+        in_specs=[
+            pl.BlockSpec(memory_space=pltpu.SMEM),
+            pl.BlockSpec(memory_space=pltpu.VMEM),
+            pl.BlockSpec(memory_space=pltpu.VMEM),
+        ],
+        out_shape=[jax.ShapeDtypeStruct((7, w), jnp.float32) for w in widths],
+    )(counts, payload, cells)
+
+
 def combine(total):
     total = total.reshape(SPLITS, 4, ROWS * COLS)
     summed = (total[0] + total[1]) + total[2]
     return summed.reshape(4, NZ, CX, CY)
 
 
-def shifted(block, axis, route_to):
-    count = lax.axis_size(axis)
-    return lax.ppermute(block, axis, [(i, (i + route_to) % count) for i in range(count)])
+def towards(block, sx, sy):
+    gx = lax.axis_size("gx")
+    gy = lax.axis_size("gy")
+    route = []
+    for ix in range(gx):
+        for iy in range(gy):
+            route.append((ix * gy + iy, ((ix + sx) % gx) * gy + (iy + sy) % gy))
+    return lax.ppermute(block, ("gx", "gy"), route)
 
 
 def bordered_density(density):
-    head = density[:, :HALO, :]
-    tail = density[:, CX - HALO :, :]
-    wide = jnp.concatenate([density, shifted(head, "gx", -1), shifted(tail, "gx", 1)], axis=1)
-    head = wide[:, :, :HALO]
-    tail = wide[:, :, CY - HALO :]
+    low_x, high_x = slice(0, HALO), slice(CX - HALO, CX)
+    low_y, high_y = slice(0, HALO), slice(CY - HALO, CY)
+    every = slice(None)
+    upper_x = towards(density[:, low_x, :], -1, 0)
+    lower_x = towards(density[:, high_x, :], 1, 0)
+    upper_y = towards(density[:, :, low_y], 0, -1)
+    lower_y = towards(density[:, :, high_y], 0, 1)
+    upper_both = towards(density[:, low_x, low_y], -1, -1)
+    upper_lower = towards(density[:, low_x, high_y], -1, 1)
+    lower_upper = towards(density[:, high_x, low_y], 1, -1)
+    lower_both = towards(density[:, high_x, high_y], 1, 1)
+    wide = jnp.concatenate([density, upper_x, lower_x], axis=1)
+    right = jnp.concatenate([upper_y, upper_both, lower_upper], axis=1)
+    left = jnp.concatenate([lower_y, upper_lower, lower_both], axis=1)
     gap = jnp.zeros((NZ, WIDE_X, WIDE_Y - CY - 2 * HALO), jnp.float32)
-    return jnp.concatenate([wide, shifted(head, "gy", -1), gap, shifted(tail, "gy", 1)], axis=2)
+    return jnp.concatenate([wide, right, gap, left], axis=2)
 
 
 def near(v):
@@ -162,28 +220,11 @@
 
 
 def shards(payload, cells, counts):
-    tallies = counts[0]
-    limits = jnp.cumsum(tallies)
-    starts = limits - tallies
-    packed = jnp.concatenate([payload, cells.astype(jnp.float32)], axis=0)
-
-    gx = lax.axis_size("gx")
-    gy = lax.axis_size("gy")
-    sends = []
-    for which, (sx, sy) in enumerate(STEPS):
-        capacity = CAP_F if which < 4 else CAP_D
-        block = lax.dynamic_slice_in_dim(packed, starts[which], capacity, 1)
-        living = (jnp.arange(capacity, dtype=jnp.int32) < tallies[which]).astype(jnp.float32)
-        block = jnp.concatenate([block[0:1] * living[None, :], block[1:]], axis=0)
-        route = []
-        for ix in range(gx):
-            for iy in range(gy):
-                route.append((ix * gy + iy, ((ix + sx) % gx) * gy + (iy + sy) % gy))
-        sends.append(lax.ppermute(block, ("gx", "gy"), route))
-
-    total = deposit(payload, cells, starts[8].reshape(1))
+    blocks = pack(payload, cells, counts)
+    sends = [towards(block, sx, sy) for block, (sx, sy) in zip(blocks, STEPS)]
+    total = deposit(payload, cells, counts, local_start, BLOCK)
     arrived = jnp.concatenate(sends, axis=1)
-    total = deposit(arrived[0:4], arrived[4:7], jnp.zeros((1,), jnp.int32), total)
+    total = deposit(arrived[0:4], arrived[4:7], counts, no_start, ARRIVED_BLOCK, total)
     interior = combine(total)
     density = interior[0]
     momentum = interior[1:]

time: 93.3 us -> 77.4 us (0.83)
  between operations: 16 us -> 0.78 us
  starting transfers between devices: 31.1 us -> 41.3 us
  other arithmetic: 8.86 us -> 1.96 us
  waiting for transfers between devices: 14.6 us -> 9.4 us
  Pallas kernels: 17.8 us -> 21.6 us
  local copies, waits for them, and re-layouts: 4.43 us -> 2.45 us
    ppermute x12 -> x16, starting transfers between devices: 31.1 us -> 41.3 us  [towards(): return lax.ppermute(block, ('gx', 'gy'), route)]
    mul x8 -> x0, other arithmetic: 5.23 us -> none  [shards(): block = jnp.concatenate([block[0:1] * living[None, :], block[1:]], axis=0)]
    ppermute x12 -> x16, waiting for transfers between devices: 14.6 us -> 9.4 us  [towards(): return lax.ppermute(block, ('gx', 'gy'), route)]
    pallas_call x2, Pallas kernels: 14.2 us -> 16.2 us  [deposit(): pl.pallas_call(kernel, grid_spec=pltpu.PrefetchScalarGridSpec(num_scalar_...]
    pallas_call x0 -> x1, Pallas kernels: none -> 1.83 us  [pack(): pl.pallas_call(pack_kernel, in_specs=[pl.BlockSpec(memory_space=pltpu.SME...]
    slice x12 -> x3, local copies, waits for them, and re-layouts: 1.53 us -> 0.16 us  [the longest x1 0.08 us: bordered_density(): upper_both = towards(density[:, low_x, low_y], -1, -1)]
    convert_element_type x1 -> x0, other arithmetic: 1.04 us -> none  [shards(): packed = jnp.concatenate([payload, cells.astype(jnp.float32)], axis=0)]
  transfers between devices with their start and end apart: 12 -> 16, of which waited for: 5 -> 2; matrix products, arithmetic and copies ran while one was open for 6% -> 1% of each run, Pallas kernels for 7% -> 10%
where the time goes in v1:
time: 77.4 us; the launch traced here: 77.5 us
  starting transfers between devices  41.3 us (53%)
  Pallas kernels  21.6 us (28%)
  waiting for transfers between devices  9.4 us (12%)
  local copies, waits for them, and re-layouts  2.45 us (3%)
  other arithmetic  1.96 us (3%)
  between operations  0.78 us (1%)
    ppermute x16, starting transfers between devices, towards(): return lax.ppermute(block, ('gx', 'gy'), route)  41.3 us
    pallas_call x2, Pallas kernels, deposit(): pl.pallas_call(kernel, grid_spec=pltpu.PrefetchScalarGridSpec(num_scalar_...  16.2 us
    ppermute x16, waiting for transfers between devices, towards(): return lax.ppermute(block, ('gx', 'gy'), route)  9.4 us
    pallas_call x1, Pallas kernels, relax(): pl.pallas_call(relax_kernel, out_shape=jax.ShapeDtypeStruct((NZ, CX, CY),...  3.56 us
    pallas_call x1, Pallas kernels, pack(): pl.pallas_call(pack_kernel, in_specs=[pl.BlockSpec(memory_space=pltpu.SME...  1.83 us
  transfers between devices with their start and end apart: 16, of which 2 were waited for; matrix products, arithmetic and copies ran while one was open for 1% of the time, Pallas kernels for 10%

profile of v1, /device:TPU:0, one launch (start us, length us, event | category | flops | bytes accessed | tf_op | source)
XLA Modules:
  0.0 77.5 jit_solution(3523996867644390381)
XLA Ops:
  0.6 1.8 %shard_map.50 = (f32[7,2176]{1,0:T(8,128)}, f32[7,2176]{1,0:T(8,128)}, f32[7,2176]{1,0:T(8,128)}, f32[7,2176]{1,0:T(8,128)}, f32[7,640]{1,0:T(8,128)}, /*index=5...) custom-call(s32[1,9]{1,0:T(1,128)} %f.3, f32[4,16384]{1,0:T(4,128)} %p.1, s32[3,16384]{1,0:T(4,128)} %c.1), custom_call_target="tpu_custom_call" | custom-call | tf_op jit(solution)/shard_map/pallas_call | solution.py:130
  2.5 6.3 %collective-permute-start.1 = (f32[7,2176]{1,0:T(8,128)}, f32[7,2176]{1,0:T(8,128)S(1)}, u32[]{:S(2)}, u32[]{:S(2)}) collective-permute-start(f32[7,2176]{1,0:T(8,128)} %get-tuple-element.11), channel_id=1, source_target_pairs={{0,120},{1,121},{2,122},{3,123},{4,124},{5,125},{6,126},{7,127},{8... | collective-permute-start | bytes 182792 | tf_op jit(solution)/shard_map/ppermute | solution.py:154
  8.8 0.7 collective-permute-start.2
  9.6 3.4 %collective-permute-start.3 = (f32[7,2176]{1,0:T(8,128)}, f32[7,2176]{1,0:T(8,128)S(1)}, u32[]{:S(2)}, u32[]{:S(2)}) collective-permute-start(f32[7,2176]{1,0:T(8,128)} %get-tuple-element.13), channel_id=1, source_target_pairs={{0,7},{1,0},{2,1},{3,2},{4,3},{5,4},{6,5},{7,6},{8,15},{9,8},{10,9... | collective-permute-start | bytes 182792 | tf_op jit(solution)/shard_map/ppermute | solution.py:154
  13.0 8.0 %shard_map.51.a = f32[768,256]{1,0:T(8,128)} custom-call(s32[1,9]{1,0:T(1,128)} %f.3, f32[4,16384]{1,0:T(4,128)} %p.1, s32[3,16384]{1,0:T(4,128)} %c.1), custom_call_target="tpu_custom_call" | custom-call | tf_op jit(solution)/shard_map/pallas_call | solution.py:97
  20.9 0.7 collective-permute-start.5
  21.7 4.6 %collective-permute-start.6 = (f32[7,640]{1,0:T(8,128)S(1)}, f32[7,640]{1,0:T(8,128)S(1)}, u32[]{:S(2)}, u32[]{:S(2)}) collective-permute-start(f32[7,640]{1,0:T(8,128)S(1)} %copy-done.1), channel_id=1, source_target_pairs={{0,121},{1,122},{2,123},{3,124},{4,125},{5,126},{6,127},{7,120},{8... | collective-permute-start | bytes 53768 | tf_op jit(solution)/shard_map/ppermute | solution.py:154
  26.3 5.8 %collective-permute-start.7 = (f32[7,640]{1,0:T(8,128)S(1)}, f32[7,640]{1,0:T(8,128)S(1)}, u32[]{:S(2)}, u32[]{:S(2)}) collective-permute-start(f32[7,640]{1,0:T(8,128)S(1)} %copy-done), channel_id=1, source_target_pairs={{0,127},{1,120},{2,121},{3,122},{4,123},{5,124},{6,125},{7,126},{8... | collective-permute-start | bytes 53768 | tf_op jit(solution)/shard_map/ppermute | solution.py:154
  32.2 1.4 %collective-permute-done.7 = f32[7,640]{1,0:T(8,128)S(1)} collective-permute-done((f32[7,640]{1,0:T(8,128)S(1)}, f32[7,640]{1,0:T(8,128)S(1)}, u32[]{:S(2)}, u32[]{:S(2)}) %collective-permute-start.7) | collective-permute-done | bytes 17952 | tf_op jit(solution)/shard_map/ppermute | solution.py:154
  33.6 0.7 slice.70.p
  34.3 0.7 slice.71.c
  35.0 8.2 %shard_map.52 = f32[768,256]{1,0:T(8,128)} custom-call(s32[1,9]{1,0:T(1,128)} %f.3, f32[4,11264]{1,0:T(4,128)} %slice.70.p, f32[3,11264]{1,0:T(4,128)} %slice.71.c, f32[768,256]{1,0:T(8,128)} %shard_map.51.a), custom_call_target="tpu_custom_call", output_to_operand_aliasing={{}: (3, {})} | custom-call | tf_op jit(solution)/shard_map/pallas_call | solution.py:97
  43.2 1.2 %slice_add_fusion = f32[256,256]{1,0:T(8,128)S(1)} fusion(f32[768,256]{1,0:T(8,128)} %shard_map.52), kind=kLoop, calls=%fused_computation | loop fusion | flops 131072 | bytes 1048576 | tf_op jit(solution)/shard_map/add | solution.py:143
  44.4 0.1 fusion.2
  44.5 7.2 %collective-permute-start.11 = (f32[8,8,8]{2,1,0:T(8,128)S(1)}, f32[8,8,8]{2,1,0:T(8,128)S(1)}, u32[]{:S(2)}, u32[]{:S(2)}) collective-permute-start(f32[8,8,8]{2,1,0:T(8,128)S(1)} %get-tuple-element.22), channel_id=1, source_target_pairs={{0,127},{1,120},{2,121},{3,122},{4,123},{5,124},{6,125},{7,126},{8... | collective-permute-start | bytes 6152 | tf_op jit(solution)/shard_map/ppermute | solution.py:154
  51.8 0.5 collective-permute-start.9
  52.3 0.1 fusion.1
  52.3 9.9 %collective-permute-start.14 = (f32[8,8,8]{2,1,0:T(8,128)S(1)}, f32[8,8,8]{2,1,0:T(8,128)S(1)}, u32[]{:S(2)}, u32[]{:S(2)}) collective-permute-start(f32[8,8,8]{2,1,0:T(8,128)S(1)} %get-tuple-element.24), channel_id=1, source_target_pairs={{0,121},{1,122},{2,123},{3,124},{4,125},{5,126},{6,127},{7,120},{8... | collective-permute-start | bytes 6152 | tf_op jit(solution)/shard_map/ppermute | solution.py:154
  62.3 2.0 %collective-permute-start.13 = (f32[8,16,8]{2,1,0:T(8,128)S(1)}, f32[8,16,8]{2,1,0:T(8,128)S(1)}, u32[]{:S(2)}, u32[]{:S(2)}) collective-permute-start(f32[8,16,8]{2,1,0:T(8,128)S(1)} %get-tuple-element.21), channel_id=1, source_target_pairs={{0,1},{1,2},{2,3},{3,4},{4,5},{5,6},{6,7},{7,0},{8,9},{9,10},{10,1... | collective-permute-start | bytes 12296 | tf_op jit(solution)/shard_map/ppermute | solution.py:154
  64.3 0.1 pad.6.clone
  64.4 0.7 slice.69
  65.1 8.0 %collective-permute-done.15 = f32[8,8,8]{2,1,0:T(8,128)S(1)} collective-permute-done((f32[8,8,8]{2,1,0:T(8,128)S(1)}, f32[8,8,8]{2,1,0:T(8,128)S(1)}, u32[]{:S(2)}, u32[]{:S(2)}) %collective-permute-start.15) | collective-permute-done | bytes 2080 | tf_op jit(solution)/shard_map/ppermute | solution.py:154
  73.1 0.8 %maximum_maximum_fusion.d_ref = f32[8,32,256]{2,1,0:T(8,128)} fusion(f32[8,8,8]{2,1,0:T(8,128)S(1)} %collective-permute-done.15, f32[8,8,8]{2,1,0:T(8,128)S(1)} %collective-permute-done.14, f32[8,16,8]{2,1,0:T(8,128)S(1)} %collective-permute-done.13, f32[8,8,8]{2,1,0:T(8,128)S(1)} %collective-permute-done.12, f32[8,8,8]{2,1,0:T(8,128)S(1)} %collective-permute-done.11, ...), kind=kLoop, calls=%fused_computation.2 | loop fusion | flops 589824 | bytes 410624 | tf_op jit(solution)/shard_map/concatenate | solution.py:173
  73.9 3.6 %shard_map.53 = f32[8,16,128]{2,1,0:T(8,128)} custom-call(f32[8,32,256]{2,1,0:T(8,128)} %maximum_maximum_fusion.d_ref), custom_call_target="tpu_custom_call" | custom-call | tf_op jit(solution)/shard_map/pallas_call | solution.py:216
  (39 shorter events, 0.2 us)
Async XLA Ops:
  2.5 18.5 %collective-permute-start = (f32[7,2176]{1,0:T(8,128)}, f32[7,2176]{1,0:T(8,128)S(1)}, u32[]{:S(2)}, u32[]{:S(2)}) collective-permute-start(f32[7,2176]{1,0:T(8,128)} %get-tuple-element.10), channel_id=1, source_target_pairs={{0,8},{1,9},{2,10},{3,11},{4,12},{5,13},{6,14},{7,15},{8,16},{9,17... | collective-permute-start | bytes 182792 | tf_op jit(solution)/shard_map/ppermute | solution.py:154
  2.5 19.1 %collective-permute-start.1 = (f32[7,2176]{1,0:T(8,128)}, f32[7,2176]{1,0:T(8,128)S(1)}, u32[]{:S(2)}, u32[]{:S(2)}) collective-permute-start(f32[7,2176]{1,0:T(8,128)} %get-tuple-element.11), channel_id=1, source_target_pairs={{0,120},{1,121},{2,122},{3,123},{4,124},{5,125},{6,126},{7,127},{8... | collective-permute-start | bytes 182792 | tf_op jit(solution)/shard_map/ppermute | solution.py:154
  8.8 17.5 %collective-permute-start.2 = (f32[7,2176]{1,0:T(8,128)}, f32[7,2176]{1,0:T(8,128)S(1)}, u32[]{:S(2)}, u32[]{:S(2)}) collective-permute-start(f32[7,2176]{1,0:T(8,128)} %get-tuple-element.12), channel_id=1, source_target_pairs={{0,1},{1,2},{2,3},{3,4},{4,5},{5,6},{6,7},{7,0},{8,9},{9,10},{10,1... | collective-permute-start | bytes 182792 | tf_op jit(solution)/shard_map/ppermute | solution.py:154
  9.6 22.5 %collective-permute-start.3 = (f32[7,2176]{1,0:T(8,128)}, f32[7,2176]{1,0:T(8,128)S(1)}, u32[]{:S(2)}, u32[]{:S(2)}) collective-permute-start(f32[7,2176]{1,0:T(8,128)} %get-tuple-element.13), channel_id=1, source_target_pairs={{0,7},{1,0},{2,1},{3,2},{4,3},{5,4},{6,5},{7,6},{8,15},{9,8},{10,9... | collective-permute-start | bytes 182792 | tf_op jit(solution)/shard_map/ppermute | solution.py:154
  13.0 8.0 %copy-start.2 = (f32[7,640]{1,0:T(8,128)S(1)}, f32[7,640]{1,0:T(8,128)}, u32[]{:S(2)}) copy-start(f32[7,640]{1,0:T(8,128)} %get-tuple-element.15) | copy-start | bytes 53764
  13.0 19.2 %collective-permute-start.4 = (f32[7,640]{1,0:T(8,128)}, f32[7,640]{1,0:T(8,128)S(1)}, u32[]{:S(2)}, u32[]{:S(2)}) collective-permute-start(f32[7,640]{1,0:T(8,128)} %get-tuple-element.14), channel_id=1, source_target_pairs={{0,9},{1,10},{2,11},{3,12},{4,13},{5,14},{6,15},{7,8},{8,17},{9,18... | collective-permute-start | bytes 53768 | tf_op jit(solution)/shard_map/ppermute | solution.py:154
  20.9 0.7 copy-start.1
  20.9 11.2 %collective-permute-start.5 = (f32[7,640]{1,0:T(8,128)S(1)}, f32[7,640]{1,0:T(8,128)S(1)}, u32[]{:S(2)}, u32[]{:S(2)}) collective-permute-start(f32[7,640]{1,0:T(8,128)S(1)} %copy-done.2), channel_id=1, source_target_pairs={{0,15},{1,8},{2,9},{3,10},{4,11},{5,12},{6,13},{7,14},{8,23},{9,16... | collective-permute-start | bytes 53768 | tf_op jit(solution)/shard_map/ppermute | solution.py:154
  21.7 4.7 %copy-start = (f32[7,640]{1,0:T(8,128)S(1)}, f32[7,640]{1,0:T(8,128)}, u32[]{:S(2)}) copy-start(f32[7,640]{1,0:T(8,128)} %get-tuple-element.17) | copy-start | bytes 53764
  21.7 10.5 %collective-permute-start.6 = (f32[7,640]{1,0:T(8,128)S(1)}, f32[7,640]{1,0:T(8,128)S(1)}, u32[]{:S(2)}, u32[]{:S(2)}) collective-permute-start(f32[7,640]{1,0:T(8,128)S(1)} %copy-done.1), channel_id=1, source_target_pairs={{0,121},{1,122},{2,123},{3,124},{4,125},{5,126},{6,127},{7,120},{8... | collective-permute-start | bytes 53768 | tf_op jit(solution)/shard_map/ppermute | solution.py:154
  26.3 7.2 %collective-permute-start.7 = (f32[7,640]{1,0:T(8,128)S(1)}, f32[7,640]{1,0:T(8,128)S(1)}, u32[]{:S(2)}, u32[]{:S(2)}) collective-permute-start(f32[7,640]{1,0:T(8,128)S(1)} %copy-done), channel_id=1, source_target_pairs={{0,127},{1,120},{2,121},{3,122},{4,123},{5,124},{6,125},{7,126},{8... | collective-permute-start | bytes 53768 | tf_op jit(solution)/shard_map/ppermute | solution.py:154
  44.5 17.8 %collective-permute-start.11 = (f32[8,8,8]{2,1,0:T(8,128)S(1)}, f32[8,8,8]{2,1,0:T(8,128)S(1)}, u32[]{:S(2)}, u32[]{:S(2)}) collective-permute-start(f32[8,8,8]{2,1,0:T(8,128)S(1)} %get-tuple-element.22), channel_id=1, source_target_pairs={{0,127},{1,120},{2,121},{3,122},{4,123},{5,124},{6,125},{7,126},{8... | collective-permute-start | bytes 6152 | tf_op jit(solution)/shard_map/ppermute | solution.py:154
  51.7 10.6 %collective-permute-start.12 = (f32[8,8,8]{2,1,0:T(8,128)S(1)}, f32[8,8,8]{2,1,0:T(8,128)S(1)}, u32[]{:S(2)}, u32[]{:S(2)}) collective-permute-start(f32[8,8,8]{2,1,0:T(8,128)S(1)} %get-tuple-element.25), channel_id=1, source_target_pairs={{0,15},{1,8},{2,9},{3,10},{4,11},{5,12},{6,13},{7,14},{8,23},{9,16... | collective-permute-start | bytes 6152 | tf_op jit(solution)/shard_map/ppermute | solution.py:154
  51.7 21.4 %collective-permute-start.8 = (f32[8,8,128]{2,1,0:T(8,128)S(1)}, f32[8,8,128]{2,1,0:T(8,128)S(1)}, u32[]{:S(2)}, u32[]{:S(2)}) collective-permute-start(f32[8,8,128]{2,1,0:T(8,128)S(1)} %get-tuple-element.18), channel_id=1, source_target_pairs={{0,120},{1,121},{2,122},{3,123},{4,124},{5,125},{6,126},{7,127},{8... | collective-permute-start | bytes 98312 | tf_op jit(solution)/shard_map/ppermute | solution.py:154
  51.8 21.4 %collective-permute-start.9 = (f32[8,8,128]{2,1,0:T(8,128)S(1)}, f32[8,8,128]{2,1,0:T(8,128)S(1)}, u32[]{:S(2)}, u32[]{:S(2)}) collective-permute-start(f32[8,8,128]{2,1,0:T(8,128)S(1)} %get-tuple-element.19), channel_id=1, source_target_pairs={{0,8},{1,9},{2,10},{3,11},{4,12},{5,13},{6,14},{7,15},{8,16},{9,17... | collective-permute-start | bytes 98312 | tf_op jit(solution)/shard_map/ppermute | solution.py:154
  52.3 12.0 %collective-permute-start.14 = (f32[8,8,8]{2,1,0:T(8,128)S(1)}, f32[8,8,8]{2,1,0:T(8,128)S(1)}, u32[]{:S(2)}, u32[]{:S(2)}) collective-permute-start(f32[8,8,8]{2,1,0:T(8,128)S(1)} %get-tuple-element.24), channel_id=1, source_target_pairs={{0,121},{1,122},{2,123},{3,124},{4,125},{5,126},{6,127},{7,120},{8... | collective-permute-start | bytes 6152 | tf_op jit(solution)/shard_map/ppermute | solution.py:154
  62.3 10.8 %collective-permute-start.10 = (f32[8,16,8]{2,1,0:T(8,128)S(1)}, f32[8,16,8]{2,1,0:T(8,128)S(1)}, u32[]{:S(2)}, u32[]{:S(2)}) collective-permute-start(f32[8,16,8]{2,1,0:T(8,128)S(1)} %get-tuple-element.20), channel_id=1, source_target_pairs={{0,7},{1,0},{2,1},{3,2},{4,3},{5,4},{6,5},{7,6},{8,15},{9,8},{10,9... | collective-permute-start | bytes 12296 | tf_op jit(solution)/shard_map/ppermute | solution.py:154
  62.3 10.8 %collective-permute-start.13 = (f32[8,16,8]{2,1,0:T(8,128)S(1)}, f32[8,16,8]{2,1,0:T(8,128)S(1)}, u32[]{:S(2)}, u32[]{:S(2)}) collective-permute-start(f32[8,16,8]{2,1,0:T(8,128)S(1)} %get-tuple-element.21), channel_id=1, source_target_pairs={{0,1},{1,2},{2,3},{3,4},{4,5},{5,6},{6,7},{7,0},{8,9},{9,10},{10,1... | collective-permute-start | bytes 12296 | tf_op jit(solution)/shard_map/ppermute | solution.py:154
  64.3 8.8 %collective-permute-start.15 = (f32[8,8,8]{2,1,0:T(8,128)S(1)}, f32[8,8,8]{2,1,0:T(8,128)S(1)}, u32[]{:S(2)}, u32[]{:S(2)}) collective-permute-start(f32[8,8,8]{2,1,0:T(8,128)S(1)} %get-tuple-element.23), channel_id=1, source_target_pairs={{0,9},{1,10},{2,11},{3,12},{4,13},{5,14},{6,15},{7,8},{8,17},{9,18... | collective-permute-start | bytes 6152 | tf_op jit(solution)/shard_map/ppermute | solution.py:154
